TPU v7x, 32 devices: a whole 2x2x4 slice. The times are simulated.
32 devices in a mesh: outer: 4 (over y, x), inner: 8 (over z, core).
Axes of the slice: x: 2, y: 2, z: 4, core: 2. Of those that a mesh axis runs over, the one named last changes fastest.
Arguments:
- tokens: bfloat16 [4096, 2048], P(('outer', 'inner')), may hold values from -6 to 6
- cotangent: bfloat16 [4096, 2048], P(('outer', 'inner')), may hold values from -6 to 6
- routes: int32 [4096, 8], P(('outer', 'inner')), may hold values from 0 to 31, all different within a row; in each aligned block of 128 rows (0 to 127, 128 to 255, ...) at most 36 rows name the same one
- router_weight: bfloat16 [2048, 32], replicated, may hold values from -0.125 to 0.125
- gate_saved: bfloat16 [32, 1152, 768], P(('outer', 'inner')), may hold values from -6 to 6
- up_saved: bfloat16 [32, 1152, 768], P(('outer', 'inner')), may hold values from -6 to 6
- gate_weight: bfloat16 [32, 2048, 768], P(('outer', 'inner')), may hold values from -0.125 to 0.125
- up_weight: bfloat16 [32, 2048, 768], P(('outer', 'inner')), may hold values from -0.125 to 0.125
- down_weight: bfloat16 [32, 768, 2048], P(('outer', 'inner')), may hold values from -0.21875 to 0.21875
Outputs:
- grad_tokens: bfloat16 [4096, 2048], P(('outer', 'inner'))
- grad_gate: bfloat16 [32, 2048, 768], P(('outer', 'inner'))
- grad_up: bfloat16 [32, 2048, 768], P(('outer', 'inner'))
- grad_down: bfloat16 [32, 768, 2048], P(('outer', 'inner'))
- grad_router: float32 [2048, 32], replicated
Inputs may be any that keep to these rules, and one draw needn't show every extreme that they name: `routes`: each row names 8 different experts. Among the rows of one device no expert is named more than 36 times, and in every draw some expert is named exactly 36 times by the rows of some device.
All inputs are finite; a program needn't handle non-finite values.
Results may differ from a plain program's by a relative error of at most 0.01.
Values may be sent and summed in bfloat16 or wider, within the bound.
No kernel may reach another device: no remote copies, remote signals or barrier semaphores. Data moves between devices by JAX's collectives and lax.ppermute only.
A program may use at most 192 MiB of HBM per device.

v0:
```python
import math
import jax
import jax.numpy as jnp
from jax import lax
from jax.sharding import PartitionSpec as P

contract_rows = (((0,), (0,)), ((), ()))
contract_cols = (((1,), (1,)), ((), ()))


def route_tables(routes, experts, capacity):
    flat_routes = routes.reshape(-1)
    onehot = (flat_routes[:, None] == jnp.arange(experts, dtype=jnp.int32)[None, :]).astype(
        jnp.int32
    )
    pairs = flat_routes.shape[0]
    lower = (
        jnp.arange(pairs, dtype=jnp.int32)[:, None] > jnp.arange(pairs, dtype=jnp.int32)[None, :]
    ).astype(jnp.bfloat16)
    earlier = jnp.dot(
        lower, onehot.astype(jnp.bfloat16), preferred_element_type=jnp.float32
    ).astype(jnp.int32)
    position = jnp.sum(earlier * onehot, axis=1)
    target = flat_routes * capacity + position
    slot_table = (
        jnp.arange(experts * capacity, dtype=jnp.int32)[:, None] == target[None, :]
    ).astype(jnp.bfloat16)
    token_table = jnp.sum(
        slot_table.reshape(experts * capacity, routes.shape[0], routes.shape[1]), axis=2
    )
    return (slot_table, token_table)


def route_probs(tokens, routes, router_weight):
    router_logits = jnp.dot(tokens, router_weight, preferred_element_type=jnp.float32)
    picked = (
        routes[:, :, None] == jnp.arange(router_weight.shape[1], dtype=jnp.int32)[None, None, :]
    )
    chosen = jnp.sum(jnp.where(picked, router_logits[:, None, :], jnp.float32(0.0)), axis=2)
    exp_terms = jnp.exp(chosen)
    return (picked, exp_terms / jnp.sum(exp_terms, axis=1, keepdims=True))


def dispatch_block(tokens, cotangent, routes, router_weight, capacity):
    picked, probs = route_probs(tokens, routes, router_weight)
    slot_table, token_table = route_tables(routes, router_weight.shape[1], capacity)
    send_tokens = jnp.dot(token_table, tokens, preferred_element_type=jnp.float32).astype(
        jnp.bfloat16
    )
    send_cot = jnp.dot(token_table, cotangent, preferred_element_type=jnp.float32).astype(
        jnp.bfloat16
    )
    probs_low = probs.astype(jnp.bfloat16).reshape(-1)
    send_weight = jnp.dot(slot_table, probs_low, preferred_element_type=jnp.float32).astype(
        jnp.bfloat16
    )
    return (picked, probs, slot_table, token_table, send_tokens, send_cot, send_weight)


def slot_dot(cot_rows, out_rows):
    return jnp.sum(cot_rows.astype(jnp.float32) * out_rows.astype(jnp.float32), axis=1).astype(
        jnp.bfloat16
    )


def expert_backward(
    input_rows, cot_rows, weight_rows, gate_pre, up_pre, gate_matrix, up_matrix, down_matrix
):
    gate_value = gate_pre.astype(jnp.float32)
    up_value = up_pre.astype(jnp.float32)
    sigmoid_gate = jax.nn.sigmoid(gate_value)
    silu_gate = gate_value * sigmoid_gate
    hidden = (silu_gate * up_value).astype(jnp.bfloat16)
    expert_out = jnp.dot(hidden, down_matrix, preferred_element_type=jnp.float32).astype(
        jnp.bfloat16
    )
    scaled_cot = (weight_rows.astype(jnp.float32)[:, None] * cot_rows.astype(jnp.float32)).astype(
        jnp.bfloat16
    )
    grad_hidden = lax.dot_general(
        scaled_cot, down_matrix, contract_cols, preferred_element_type=jnp.float32
    )
    grad_gate_pre = (
        grad_hidden * up_value * sigmoid_gate * (1.0 + gate_value * (1.0 - sigmoid_gate))
    ).astype(jnp.bfloat16)
    grad_up_pre = (grad_hidden * silu_gate).astype(jnp.bfloat16)
    grad_rows = (
        lax.dot_general(
            grad_gate_pre, gate_matrix, contract_cols, preferred_element_type=jnp.float32
        )
        + lax.dot_general(grad_up_pre, up_matrix, contract_cols, preferred_element_type=jnp.float32)
    ).astype(jnp.bfloat16)
    grad_gate_w = lax.dot_general(
        input_rows, grad_gate_pre, contract_rows, preferred_element_type=jnp.float32
    ).astype(jnp.bfloat16)
    grad_up_w = lax.dot_general(
        input_rows, grad_up_pre, contract_rows, preferred_element_type=jnp.float32
    ).astype(jnp.bfloat16)
    grad_down_w = lax.dot_general(
        hidden, scaled_cot, contract_rows, preferred_element_type=jnp.float32
    ).astype(jnp.bfloat16)
    return (grad_rows, expert_out, grad_gate_w, grad_up_w, grad_down_w)


def finish_block(
    tokens, router_weight, picked, probs, slot_table, token_table, back_rows, route_dot
):
    grad_sum = lax.dot_general(
        token_table, back_rows, contract_rows, preferred_element_type=jnp.float32
    )
    route_grad = lax.dot_general(
        slot_table, route_dot, contract_rows, preferred_element_type=jnp.float32
    ).reshape(probs.shape)
    inner_term = jnp.sum(probs * route_grad, axis=1, keepdims=True)
    chosen_grad = probs * (route_grad - inner_term)
    logit_grad = jnp.sum(
        jnp.where(picked, chosen_grad[:, :, None], jnp.float32(0.0)), axis=1
    ).astype(jnp.bfloat16)
    grad_tokens = (
        grad_sum
        + lax.dot_general(
            logit_grad, router_weight, contract_cols, preferred_element_type=jnp.float32
        )
    ).astype(jnp.bfloat16)
    router_part = lax.dot_general(
        tokens, logit_grad, contract_rows, preferred_element_type=jnp.float32
    )
    return (grad_tokens, router_part)


def body(
    tokens,
    cotangent,
    routes,
    router_weight,
    gate_saved,
    up_saved,
    gate_weight,
    up_weight,
    down_weight,
):
    experts = router_weight.shape[1]
    width = tokens.shape[1]
    capacity = gate_saved.shape[1] // experts
    outer_size = lax.axis_size("outer")
    inner_size = lax.axis_size("inner")
    axes = ("outer", "inner")
    picked, probs = route_probs(tokens, routes, router_weight)
    slot_table, token_table = route_tables(routes, experts, capacity)
    both = jnp.concatenate([tokens, cotangent], axis=1)
    grid_both = jnp.dot(
        token_table.reshape(experts, capacity, -1), both, preferred_element_type=jnp.float32
    ).astype(jnp.bfloat16)
    probs_low = probs.astype(jnp.bfloat16).reshape(-1)
    send_weight = jnp.dot(slot_table, probs_low, preferred_element_type=jnp.float32).astype(
        jnp.bfloat16
    )
    grid_weight = send_weight.reshape(experts, capacity)
    got_both = lax.all_to_all(grid_both, axes, split_axis=0, concat_axis=0, tiled=True)
    got_weight = lax.all_to_all(grid_weight, axes, split_axis=0, concat_axis=0, tiled=True)
    got_both = got_both.reshape(-1, 2 * width)
    input_rows = got_both[:, :width]
    cot_rows = got_both[:, width:]
    grad_rows, expert_out, grad_gate_w, grad_up_w, grad_down_w = expert_backward(
        input_rows,
        cot_rows,
        got_weight.reshape(-1),
        gate_saved[0],
        up_saved[0],
        gate_weight[0],
        up_weight[0],
        down_weight[0],
    )
    slot_route_dot = slot_dot(cot_rows, expert_out).reshape(experts, capacity)
    back_dot = lax.all_to_all(slot_route_dot, axes, split_axis=0, concat_axis=0, tiled=True)
    route_dot = back_dot.reshape(-1)
    route_grad = lax.dot_general(
        slot_table, route_dot, contract_rows, preferred_element_type=jnp.float32
    ).reshape(probs.shape)
    inner_term = jnp.sum(probs * route_grad, axis=1, keepdims=True)
    chosen_grad = probs * (route_grad - inner_term)
    logit_grad = jnp.sum(
        jnp.where(picked, chosen_grad[:, :, None], jnp.float32(0.0)), axis=1
    ).astype(jnp.bfloat16)
    router_part = lax.dot_general(
        tokens, logit_grad, contract_rows, preferred_element_type=jnp.float32
    )
    total_tokens = tokens.shape[0] * outer_size * inner_size
    grad_router = lax.psum(router_part, axes) * (1.0 / math.sqrt(total_tokens))
    back_grad = grad_rows.reshape(experts, capacity, width)
    grad_router, back_grad = lax.optimization_barrier((grad_router, back_grad))
    back_rows = lax.all_to_all(back_grad, axes, split_axis=0, concat_axis=0, tiled=True)
    grad_sum = lax.dot_general(
        token_table, back_rows.reshape(-1, width), contract_rows, preferred_element_type=jnp.float32
    )
    grad_tokens = (
        grad_sum
        + lax.dot_general(
            logit_grad, router_weight, contract_cols, preferred_element_type=jnp.float32
        )
    ).astype(jnp.bfloat16)
    return (grad_tokens, grad_gate_w[None], grad_up_w[None], grad_down_w[None], grad_router)


def solution(mesh):
    in_specs = (
        P(("outer", "inner"), None),
        P(("outer", "inner"), None),
        P(("outer", "inner"), None),
        P(),
        P(("outer", "inner"), None, None),
        P(("outer", "inner"), None, None),
        P(("outer", "inner"), None, None),
        P(("outer", "inner"), None, None),
        P(("outer", "inner"), None, None),
    )
    out_specs = (
        P(("outer", "inner"), None),
        P(("outer", "inner"), None, None),
        P(("outer", "inner"), None, None),
        P(("outer", "inner"), None, None),
        P(),
    )
    return jax.shard_map(body, mesh=mesh, in_specs=in_specs, out_specs=out_specs, check_vma=False)
```

profile of v0, /device:TPU:0, one launch (start us, length us, event | category | flops | bytes accessed | tf_op | source)
XLA Modules:
  0.0 579.3 jit_solution(17009639620150459499)
XLA Ops:
  7.2 0.0 copy-start
  7.2 0.9 copy.36
  8.1 0.1 eq.64
  8.2 0.5 fusion.62
  8.8 0.1 reduce_sum.69
  8.9 0.7 multiply_add_fusion.1
  9.6 6.0 %fusion.51 = bf16[1152,128]{1,0:T(8,128)(2,1)S(1)} fusion(s32[128,8]{0,1:T(8,128)S(1)} %multiply_add_fusion.1), kind=kLoop, calls=%fused_computation.57 | loop fusion | flops 3391488 | bytes 299008 | tf_op jit(solution)/shard_map/reduce_sum | solution.py:28
  15.6 0.8 reshape.116
  16.4 8.0 %convolution_convert_fusion = bf16[32,36,4096]{2,1,0:T(8,128)(2,1)} fusion(bf16[32,36,128]{2,1,0:T(8,128)(2,1)} %reshape.116, bf16[128,2048]{1,0:T(8,128)(2,1)} %param.10, bf16[128,2048]{1,0:T(8,128)(2,1)} %param.9), kind=kOutput, calls=%fused_computation.5 | convolution fusion | flops 1214775296 | bytes 10780672 | tf_op jit(solution)/shard_map/dot_general | solution.py:151
  24.4 7.4 %all-to-all-start = ((bf16[32,36,4096]{2,1,0:T(8,128)(2,1)}), bf16[32,36,4096]{2,1,0:T(8,128)(2,1)}, u32[]{:S(2)}, u32[]{:S(2)}) async-start(bf16[32,36,4096]{2,1,0:T(8,128)(2,1)} %convolution_convert_fusion), calls=%async_computation | async-start | bytes 20971520 | tf_op jit(solution)/shard_map/all_to_all | solution.py:159
  31.9 1.3 fusion.75
  33.2 0.0 copy-done.3
  33.3 228.5 %all-to-all-done = bf16[32,36,4096]{2,1,0:T(8,128)(2,1)} async-done(((bf16[32,36,4096]{2,1,0:T(8,128)(2,1)}), bf16[32,36,4096]{2,1,0:T(8,128)(2,1)}, u32[]{:S(2)}, u32[]{:S(2)}) %all-to-all-start) | async-done | bytes 9437216 | tf_op jit(solution)/shard_map/all_to_all | solution.py:159
  261.7 13.2 %reshape.117 = bf16[1152,4096]{1,0:T(8,128)(2,1)} reshape(bf16[32,36,4096]{2,1,0:T(8,128)(2,1)} %all-to-all-done) | data formatting | bytes 18874368 | tf_op jit(solution)/shard_map/reshape | solution.py:161
  274.9 8.6 %fusion = bf16[1152]{0:T(1024)(128)(2,1)S(1)} fusion(bf16[1152,4096]{1,0:T(8,128)(2,1)} %reshape.117, bf16[1,768,2048]{2,1,0:T(8,128)(2,1)} %param.17, bf16[1,1152,768]{2,1,0:T(8,128)(2,1)} %param.14, bf16[1,1152,768]{2,1,0:T(8,128)(2,1)} %param.13), kind=kOutput, calls=%fused_computation.2 | convolution fusion | flops 3642752000 | bytes 11405568 | tf_op jit(solution)/shard_map/dot_general | solution.py:74
  283.6 0.7 convert_element_type.152
  284.3 2.7 all-to-all-start.1
  287.1 6.9 %all-to-all-done.1 = bf16[32,1,36]{2,1,0:T(2,128)(2,1)S(1)} async-done(((bf16[32,1,36]{2,1,0:T(2,128)(2,1)}), bf16[32,1,36]{2,1,0:T(2,128)(2,1)S(1)}, u32[]{:S(2)}, u32[]{:S(2)}) %all-to-all-start.1) | async-done | bytes 2336 | tf_op jit(solution)/shard_map/all_to_all | solution.py:175
  293.9 0.1 reduce.1
  294.0 0.1 reshape.125
  294.1 5.9 %fusion.8 = f32[1,128,8]{2,0,1:T(1,128)S(1)} fusion(bf16[1152,1,1]{0,1,2:T(2,128)(2,1)S(1)} %reshape.125, s32[1024]{0:T(1024)S(1)} %multiply_add_fusion), kind=kOutput, calls=%fused_computation.19 | convolution fusion | flops 3538944 | bytes 10496 | tf_op jit(solution)/shard_map/dot_general | solution.py:177
  300.0 0.1 copy.41
  300.2 0.1 copy.39
  300.3 0.1 reshape.127
  300.4 0.9 fusion.63
  301.3 0.7 all_to_all.21
  302.0 2.5 all-to-all-start.2
  304.6 0.0 all-reduce.2.cloned.1.call-start
  304.6 2.0 convolution_bitcast_fusion
  306.6 0.0 all-reduce.2.cloned.1.call-update
  306.6 5.0 all-to-all-done.2
  311.6 0.1 convert_reduce_fusion
  311.7 0.1 reshape.121
  311.8 9.1 %fusion.19 = (bf16[1152,768]{1,0:T(8,128)(2,1)S(1)}, f32[1152,768]{1,0:T(8,128)S(1)}) fusion(bf16[1,1152,768]{2,1,0:T(8,128)(2,1)} %param.14, bf16[1,1152,768]{2,1,0:T(8,128)(2,1)} %param.13, bf16[1,768,2048]{2,1,0:T(8,128)(2,1)} %param.17, f32[1152]{0:T(1024)S(1)} %reshape.121, bf16[1152,4096]{1,0:T(8,128)(2,1)} %reshape.117), kind=kOutput, calls=%fused_computation.32 | convolution fusion | flops 3641573376 | bytes 16716288 | tf_op jit(solution)/shard_map/dot_general | solution.py:80
  321.0 6.3 %fusion.36 = f32[1152,2048]{1,0:T(8,128)} fusion(bf16[1152,768]{1,0:T(8,128)(2,1)S(1)} %get-tuple-element.11, bf16[1,2048,768]{2,1,0:T(8,128)(2,1)S(1)} %copy-done), kind=kOutput, calls=%fused_computation.47 | convolution fusion | flops 3623878656 | bytes 14352384 | tf_op jit(solution)/shard_map/dot_general | solution.py:88
  327.3 0.1 copy-done.8
  327.4 8.4 %add_convert_fusion = bf16[1152,2048]{1,0:T(8,128)(2,1)} fusion(f32[1152,2048]{1,0:T(8,128)} %fusion.36, bf16[1,2048,768]{2,1,0:T(8,128)(2,1)S(1)} %copy-done.4, f32[1152,768]{1,0:T(8,128)S(1)} %get-tuple-element.12, bf16[1,1152,768]{2,1,0:T(8,128)(2,1)S(1)} %copy-done.6), kind=kOutput, calls=%fused_computation.4 | convolution fusion | flops 3634790400 | bytes 22609920 | tf_op jit(solution)/shard_map/dot_general | solution.py:91
  335.8 7.2 %reshape.119 = bf16[32,36,2048]{2,1,0:T(8,128)(2,1)} reshape(bf16[1152,2048]{1,0:T(8,128)(2,1)} %add_convert_fusion) | data formatting | bytes 9437184 | tf_op jit(solution)/shard_map/reshape | solution.py:190
  343.0 94.8 %all-reduce.2.cloned.1.call-done = f32[2048,32]{0,1:T(8,128)} async-done(((f32[2048,32]{0,1:T(8,128)}), f32[2048,32]{0,1:T(8,128)}) %all-reduce.2.cloned.1.call-update) | async-done | bytes 262160 | tf_op jit(solution)/shard_map/psum | solution.py:189
  437.8 1.7 broadcast_multiply_fusion
  439.4 4.0 all-to-all-start.3
  443.4 9.1 %fusion.45 = bf16[1,2048,768]{2,1,0:T(8,128)(2,1)} fusion(bf16[1152,768]{1,0:T(8,128)(2,1)} %copy-done.10, bf16[1152,4096]{1,0:T(8,128)(2,1)} %reshape.117), kind=kOutput, calls=%fused_computation.54 | convolution fusion | flops 3625451520 | bytes 9633792 | tf_op jit(solution)/shard_map/dot_general | solution.py:93
  452.5 9.1 %fusion.41 = bf16[1,768,2048]{2,1,0:T(8,128)(2,1)} fusion(bf16[1,1152,768]{2,1,0:T(8,128)(2,1)S(1)} %copy-done.5, bf16[1,1152,768]{2,1,0:T(8,128)(2,1)S(1)} %copy-done.7, f32[1152]{0:T(1024)S(1)} %reshape.121, bf16[1152,4096]{1,0:T(8,128)(2,1)} %reshape.117), kind=kOutput, calls=%fused_computation.52 | convolution fusion | flops 3639607296 | bytes 11407872 | tf_op jit(solution)/shard_map/dot_general | solution.py:99
  461.7 6.3 %fusion.42 = bf16[1,2048,768]{2,1,0:T(8,128)(2,1)} fusion(bf16[1152,4096]{1,0:T(8,128)(2,1)S(1)} %bitcast.97, f32[1152,768]{1,0:T(8,128)S(1)} %copy-done.9, bf16[1,1152,768]{2,1,0:T(8,128)(2,1)S(1)} %copy-done.7), kind=kOutput, calls=%fused_computation.53 | convolution fusion | flops 3631644672 | bytes 13172736 | tf_op jit(solution)/shard_map/dot_general | solution.py:96
  468.0 92.7 %all-to-all-done.3 = bf16[32,36,2048]{2,1,0:T(8,128)(2,1)} async-done(((bf16[32,36,2048]{2,1,0:T(8,128)(2,1)}), bf16[32,36,2048]{2,1,0:T(8,128)(2,1)}, u32[]{:S(2)}, u32[]{:S(2)}) %all-to-all-start.3) | async-done | bytes 4718624 | tf_op jit(solution)/shard_map/all_to_all | solution.py:192
  560.7 7.4 %reshape.120 = bf16[1152,2048]{1,0:T(8,128)(2,1)} reshape(bf16[32,36,2048]{2,1,0:T(8,128)(2,1)} %all-to-all-done.3) | data formatting | bytes 9437184 | tf_op jit(solution)/shard_map/reshape | solution.py:194
  568.1 3.2 fusion.76
  571.3 1.1 fusion.50
  (33 shorter events, 0.2 us)
Async XLA Ops:
  7.2 313.8 %copy-start = (bf16[1,2048,768]{2,1,0:T(8,128)(2,1)S(1)}, bf16[1,2048,768]{2,1,0:T(8,128)(2,1)}, u32[]{:S(2)}) copy-start(bf16[1,2048,768]{2,1,0:T(8,128)(2,1)} %param.15) | copy-start | bytes 9437188
  24.4 8.8 %copy-start.3 = (s32[128,8]{0,1:T(8,128)S(1)}, s32[128,8]{0,1:T(8,128)}, u32[]{:S(2)}) copy-start(s32[128,8]{0,1:T(8,128)} %param.11) | copy-start | bytes 12292
  24.4 237.3 %all-to-all-start = ((bf16[32,36,4096]{2,1,0:T(8,128)(2,1)}), bf16[32,36,4096]{2,1,0:T(8,128)(2,1)}, u32[]{:S(2)}, u32[]{:S(2)}) async-start(bf16[32,36,4096]{2,1,0:T(8,128)(2,1)} %convolution_convert_fusion), calls=%async_computation | async-start | bytes 20971520 | tf_op jit(solution)/shard_map/all_to_all | solution.py:159
  284.3 9.6 %all-to-all-start.1 = ((bf16[32,1,36]{2,1,0:T(2,128)(2,1)}), bf16[32,1,36]{2,1,0:T(2,128)(2,1)S(1)}, u32[]{:S(2)}, u32[]{:S(2)}) async-start(bf16[32,1,36]{2,1,0:T(2,128)(2,1)} %convert_element_type.152), calls=%async_computation.1 | async-start | bytes 32768 | tf_op jit(solution)/shard_map/all_to_all | solution.py:175
  302.0 9.6 %all-to-all-start.2 = ((bf16[32,1,36]{2,1,0:T(2,128)(2,1)}), bf16[32,1,36]{2,1,0:T(2,128)(2,1)S(1)}, u32[]{:S(2)}, u32[]{:S(2)}) async-start(bf16[32,1,36]{2,1,0:T(2,128)(2,1)} %all_to_all.21), calls=%async_computation.2 | async-start | bytes 32768 | tf_op jit(solution)/shard_map/all_to_all | solution.py:160
  304.6 133.2 %all-reduce.2.cloned.1.call-start = ((), (), s32[]{:S(2)}) async-start(), calls=%async_computation.4 | async-start | bytes 524288 | tf_op jit(solution)/shard_map/psum | solution.py:189
  320.9 6.3 %copy-start.10 = (bf16[1152,768]{1,0:T(8,128)(2,1)}, bf16[1152,768]{1,0:T(8,128)(2,1)S(1)}, u32[]{:S(2)}) copy-start(bf16[1152,768]{1,0:T(8,128)(2,1)S(1)} %get-tuple-element.11) | copy-start | bytes 5308420
  320.9 6.4 %copy-start.8 = (f32[1152,768]{1,0:T(8,128)}, f32[1152,768]{1,0:T(8,128)S(1)}, u32[]{:S(2)}) copy-start(f32[1152,768]{1,0:T(8,128)S(1)} %get-tuple-element.12) | copy-start | bytes 10616836
  321.0 6.4 %copy-start.4 = (bf16[1,2048,768]{2,1,0:T(8,128)(2,1)S(1)}, bf16[1,2048,768]{2,1,0:T(8,128)(2,1)}, u32[]{:S(2)}) copy-start(bf16[1,2048,768]{2,1,0:T(8,128)(2,1)} %param.16) | copy-start | bytes 9437188
  321.0 6.4 %copy-start.6 = (bf16[1,1152,768]{2,1,0:T(8,128)(2,1)S(1)}, bf16[1,1152,768]{2,1,0:T(8,128)(2,1)}, u32[]{:S(2)}) copy-start(bf16[1,1152,768]{2,1,0:T(8,128)(2,1)} %param.13) | copy-start | bytes 5308420
  439.4 121.3 %all-to-all-start.3 = ((bf16[32,36,2048]{2,1,0:T(8,128)(2,1)}), bf16[32,36,2048]{2,1,0:T(8,128)(2,1)}, u32[]{:S(2)}, u32[]{:S(2)}) async-start(bf16[32,36,2048]{2,1,0:T(8,128)(2,1)} %reshape.119), calls=%async_computation.3 | async-start | bytes 10485760 | tf_op jit(solution)/shard_map/all_to_all | solution.py:192
  443.4 9.1 %copy-start.5 = (bf16[1,1152,768]{2,1,0:T(8,128)(2,1)S(1)}, bf16[1,1152,768]{2,1,0:T(8,128)(2,1)}, u32[]{:S(2)}) copy-start(bf16[1,1152,768]{2,1,0:T(8,128)(2,1)} %param.14) | copy-start | bytes 5308420
  443.4 9.1 %copy-start.7 = (bf16[1,1152,768]{2,1,0:T(8,128)(2,1)S(1)}, bf16[1,1152,768]{2,1,0:T(8,128)(2,1)}, u32[]{:S(2)}) copy-start(bf16[1,1152,768]{2,1,0:T(8,128)(2,1)} %param.13) | copy-start | bytes 5308420
  443.4 18.2 %slice-start = ((s8[9437184]{0:T(1024)(128)(4,1)}), s8[4194304]{0:T(1024)(128)(4,1)S(1)}, s32[]{:S(2)}) async-start(s8[9437184]{0:T(1024)(128)(4,1)} %bitcast.96), calls=%async_computation.5 | async-start | bytes 8388608
  443.4 18.2 %slice-start.1 = ((s8[9437184]{0:T(1024)(128)(4,1)}), s8[4194304]{0:T(1024)(128)(4,1)S(1)}, s32[]{:S(2)}) async-start(s8[9437184]{0:T(1024)(128)(4,1)} %bitcast.96), calls=%async_computation.6 | async-start | bytes 8388608
  452.5 9.1 %slice-start.2 = ((s8[9437184]{0:T(1024)(128)(4,1)}), s8[1048576]{0:T(1024)(128)(4,1)S(1)}, s32[]{:S(2)}) async-start(s8[9437184]{0:T(1024)(128)(4,1)} %bitcast.96), calls=%async_computation.7 | async-start | bytes 2097152
  452.5 9.1 %copy-start.9 = (f32[1152,768]{1,0:T(8,128)S(1)}, f32[1152,768]{1,0:T(8,128)}, u32[]{:S(2)}) copy-start(f32[1152,768]{1,0:T(8,128)} %copy-done.8) | copy-start | bytes 10616836
  560.7 11.8 %copy-start.1 = (bf16[1,2048,768]{2,1,0:T(8,128)(2,1)S(1)}, bf16[1,2048,768]{2,1,0:T(8,128)(2,1)}, u32[]{:S(2)}) copy-start(bf16[1,2048,768]{2,1,0:T(8,128)(2,1)} %param.15) | copy-start | bytes 9437188
  568.1 3.3 copy-start.2
Sparse Core Ops, SparseCore 0:
  311.5 126.2 all-reduce.1
where the time goes:
time: 580 us; the launch traced here: 579 us
  waiting for transfers between devices  428 us (74%)
  matrix products  79.9 us (14%)
  local copies, waits for them, and re-layouts  31.9 us (6%)
  starting transfers between devices  16.7 us (3%)
  between operations  14.3 us (2%)
  other arithmetic  8.64 us (1%)
    all_to_all x1, waiting for transfers between devices, body(): lax.all_to_all(grid_both, axes, split_axis=0, concat_axis=0, tiled=True)  228 us
    psum x1, waiting for transfers between devices, body(): grad_router = lax.psum(router_part, axes) * (1.0 / math.sqrt(total_tokens))  94.8 us
    all_to_all x1, waiting for transfers between devices, body(): lax.all_to_all(back_grad, axes, split_axis=0, concat_axis=0, tiled=True)  92.7 us
    reshape x1, local copies, waits for them, and re-layouts, body(): got_both = got_both.reshape(-1, 2 * width)  13.2 us
  transfers between devices with their start and end apart: 5, of which 5 were waited for; matrix products, arithmetic and copies ran while one was open for 10% of the time, Pallas kernels for 0%

commit v1 on v0

--- a/solution.py
+++ b/solution.py
@@ -186,7 +186,8 @@
         tokens, logit_grad, contract_rows, preferred_element_type=jnp.float32
     )
     total_tokens = tokens.shape[0] * outer_size * inner_size
-    grad_router = lax.psum(router_part, axes) * (1.0 / math.sqrt(total_tokens))
+    routes_all_number = lambda x_in, device_axis: lax.all_gather(x_in, device_axis).sum(axis=0)
+    grad_router = routes_all_number(router_part, device_axis=axes) * (1.0 / math.sqrt(total_tokens))
     back_grad = grad_rows.reshape(experts, capacity, width)
     grad_router, back_grad = lax.optimization_barrier((grad_router, back_grad))
     back_rows = lax.all_to_all(back_grad, axes, split_axis=0, concat_axis=0, tiled=True)

time: 580 us -> 535 us (0.922); the launches traced: 579 us -> 527 us
  waiting for transfers between devices: 428 us -> 360 us
  blocking collectives: 0 us -> 8.85 us
  local copies, waits for them, and re-layouts: 31.9 us -> 39.8 us
    psum x1 -> x0, waiting for transfers between devices: 94.8 us -> none  [body(): grad_router = lax.psum(router_part, axes) * (1.0 / math.sqrt(total_tokens))]
    all_gather x0 -> x1, waiting for transfers between devices: none -> 32.4 us  [body(): lax.all_gather(x_in, device_axis).sum(axis=0)]
    all_to_all x0 -> x1, blocking collectives: none -> 8.85 us  [body(): lax.all_to_all(grid_weight, axes, split_axis=0, concat_axis=0, tiled=True)]
    unnamed x29 -> x30, local copies, waits for them, and re-layouts: 1.12 us -> 9.44 us
  transfers between devices with their start and end apart: 5 -> 4, of which waited for: 5 -> 4; matrix products, arithmetic and copies ran while one was open for 10% -> 11% of each run, Pallas kernels for 0% -> 0%
where the time goes in v1:
time: 535 us; the launch traced here: 527 us
  waiting for transfers between devices  360 us (67%)
  matrix products  79.9 us (15%)
  local copies, waits for them, and re-layouts  39.8 us (7%)
  between operations  14.5 us (3%)
  starting transfers between devices  14.3 us (3%)
  other arithmetic  8.99 us (2%)
  blocking collectives  8.85 us (2%)
    all_to_all x1, waiting for transfers between devices, body(): lax.all_to_all(grid_both, axes, split_axis=0, concat_axis=0, tiled=True)  228 us
    all_to_all x1, waiting for transfers between devices, body(): lax.all_to_all(back_grad, axes, split_axis=0, concat_axis=0, tiled=True)  92.9 us
    all_gather x1, waiting for transfers between devices, body(): lax.all_gather(x_in, device_axis).sum(axis=0)  32.4 us
    reshape x1, local copies, waits for them, and re-layouts, body(): got_both = got_both.reshape(-1, 2 * width)  13.2 us
  transfers between devices with their start and end apart: 4, of which 4 were waited for; matrix products, arithmetic and copies ran while one was open for 11% of the time, Pallas kernels for 0%

profile of v1, /device:TPU:0, one launch (start us, length us, event | category | flops | bytes accessed | tf_op | source)
XLA Modules:
  0.0 526.6 jit_solution(7940125675408145011)
XLA Ops:
  7.2 0.9 copy.36
  8.1 0.1 eq.64
  8.2 0.5 fusion.62
  8.8 0.1 reduce_sum.78
  8.9 0.7 multiply_add_fusion.1
  9.6 6.0 %fusion.51 = bf16[1152,128]{1,0:T(8,128)(2,1)S(1)} fusion(s32[128,8]{0,1:T(8,128)S(1)} %multiply_add_fusion.1), kind=kLoop, calls=%fused_computation.58 | loop fusion | flops 3391488 | bytes 299008 | tf_op jit(solution)/shard_map/reduce_sum | solution.py:28
  15.6 0.8 reshape.116
  16.4 8.0 %convolution_convert_fusion = bf16[32,36,4096]{2,1,0:T(8,128)(2,1)} fusion(bf16[32,36,128]{2,1,0:T(8,128)(2,1)} %reshape.116, bf16[128,2048]{1,0:T(8,128)(2,1)} %param.10, bf16[128,2048]{1,0:T(8,128)(2,1)} %param.9), kind=kOutput, calls=%fused_computation.6 | convolution fusion | flops 1214775296 | bytes 10780672 | tf_op jit(solution)/shard_map/dot_general | solution.py:151
  24.4 7.4 %all-to-all-start = ((bf16[32,36,4096]{2,1,0:T(8,128)(2,1)}), bf16[32,36,4096]{2,1,0:T(8,128)(2,1)}, u32[]{:S(2)}, u32[]{:S(2)}) async-start(bf16[32,36,4096]{2,1,0:T(8,128)(2,1)} %convolution_convert_fusion), calls=%async_computation | async-start | bytes 20971520 | tf_op jit(solution)/shard_map/all_to_all | solution.py:159
  31.9 1.3 fusion.75
  33.2 0.0 copy-done.3
  33.3 228.5 %all-to-all-done = bf16[32,36,4096]{2,1,0:T(8,128)(2,1)} async-done(((bf16[32,36,4096]{2,1,0:T(8,128)(2,1)}), bf16[32,36,4096]{2,1,0:T(8,128)(2,1)}, u32[]{:S(2)}, u32[]{:S(2)}) %all-to-all-start) | async-done | bytes 9437216 | tf_op jit(solution)/shard_map/all_to_all | solution.py:159
  261.7 13.2 %reshape.117 = bf16[1152,4096]{1,0:T(8,128)(2,1)} reshape(bf16[32,36,4096]{2,1,0:T(8,128)(2,1)} %all-to-all-done) | data formatting | bytes 18874368 | tf_op jit(solution)/shard_map/reshape | solution.py:161
  274.9 8.6 %fusion = bf16[1152]{0:T(1024)(128)(2,1)S(1)} fusion(bf16[1152,4096]{1,0:T(8,128)(2,1)} %reshape.117, bf16[1,768,2048]{2,1,0:T(8,128)(2,1)} %param.17, bf16[1,1152,768]{2,1,0:T(8,128)(2,1)} %param.14, bf16[1,1152,768]{2,1,0:T(8,128)(2,1)} %param.13), kind=kOutput, calls=%fused_computation.2 | convolution fusion | flops 3642752000 | bytes 11405568 | tf_op jit(solution)/shard_map/dot_general | solution.py:74
  283.6 0.7 convert_element_type.152
  284.3 2.5 all-to-all-start.1
  286.9 0.5 all-gather.3.cloned.1.call-start
  287.4 6.5 %all-to-all-done.1 = bf16[32,1,36]{2,1,0:T(2,128)(2,1)S(1)} async-done(((bf16[32,1,36]{2,1,0:T(2,128)(2,1)}), bf16[32,1,36]{2,1,0:T(2,128)(2,1)S(1)}, u32[]{:S(2)}, u32[]{:S(2)}) %all-to-all-start.1) | async-done | bytes 2336 | tf_op jit(solution)/shard_map/all_to_all | solution.py:175
  293.9 0.1 reduce.1
  294.0 0.1 reshape.126
  294.1 5.9 %fusion.8 = f32[1,128,8]{2,0,1:T(1,128)S(1)} fusion(bf16[1152,1,1]{0,1,2:T(2,128)(2,1)S(1)} %reshape.126, s32[1024]{0:T(1024)S(1)} %multiply_add_fusion), kind=kOutput, calls=%fused_computation.20 | convolution fusion | flops 3538944 | bytes 10496 | tf_op jit(solution)/shard_map/dot_general | solution.py:177
  300.0 0.1 copy.41
  300.2 2.0 convolution_bitcast_fusion
  302.1 0.0 all-gather.3.cloned.1.call-update
  302.1 0.1 copy.39
  302.3 0.1 reshape.128
  302.4 0.9 fusion.63
  303.3 0.1 all_to_all.21
  303.4 8.8 %all_to_all.26 = bf16[32,1,36]{2,1,0:T(2,128)(2,1)S(1)} all-to-all(bf16[32,1,36]{2,1,0:T(2,128)(2,1)S(1)} %all_to_all.21), channel_id=1, replica_groups=mesh['outer'=4,'inner'=8] {'outer','inner'}, dimensions={0} | all-to-all | bytes 4608 | tf_op jit(solution)/shard_map/all_to_all | solution.py:160
  312.2 0.1 convert_reduce_fusion
  312.3 0.1 reshape.121
  312.4 9.2 %fusion.19 = (bf16[1152,768]{1,0:T(8,128)(2,1)S(1)}, f32[1152,768]{1,0:T(8,128)S(1)}) fusion(bf16[1,1152,768]{2,1,0:T(8,128)(2,1)} %param.14, bf16[1,1152,768]{2,1,0:T(8,128)(2,1)} %param.13, bf16[1,768,2048]{2,1,0:T(8,128)(2,1)} %param.17, f32[1152]{0:T(1024)S(1)} %reshape.121, bf16[1152,4096]{1,0:T(8,128)(2,1)} %reshape.117), kind=kOutput, calls=%fused_computation.33 | convolution fusion | flops 3641573376 | bytes 16716288 | tf_op jit(solution)/shard_map/dot_general | solution.py:80
  321.6 6.3 %fusion.36 = f32[1152,2048]{1,0:T(8,128)} fusion(bf16[1152,768]{1,0:T(8,128)(2,1)S(1)} %get-tuple-element.11, bf16[1,2048,768]{2,1,0:T(8,128)(2,1)S(1)} %copy-done), kind=kOutput, calls=%fused_computation.48 | convolution fusion | flops 3623878656 | bytes 14352384 | tf_op jit(solution)/shard_map/dot_general | solution.py:88
  327.9 0.1 copy-done.8
  328.0 8.3 %add_convert_fusion = bf16[1152,2048]{1,0:T(8,128)(2,1)} fusion(f32[1152,2048]{1,0:T(8,128)} %fusion.36, bf16[1,2048,768]{2,1,0:T(8,128)(2,1)S(1)} %copy-done.4, f32[1152,768]{1,0:T(8,128)S(1)} %get-tuple-element.12, bf16[1,1152,768]{2,1,0:T(8,128)(2,1)S(1)} %copy-done.6), kind=kOutput, calls=%fused_computation.4 | convolution fusion | flops 3634790400 | bytes 22609920 | tf_op jit(solution)/shard_map/dot_general | solution.py:91
  336.3 7.4 %reshape.119 = bf16[32,36,2048]{2,1,0:T(8,128)(2,1)} reshape(bf16[1152,2048]{1,0:T(8,128)(2,1)} %add_convert_fusion) | data formatting | bytes 9437184 | tf_op jit(solution)/shard_map/reshape | solution.py:191
  343.7 32.4 %all-gather.3.cloned.1.call-done = f32[65536,32]{0,1:T(8,128)} async-done(((f32[2048,32]{0,1:T(8,128)}), f32[65536,32]{0,1:T(8,128)}) %all-gather.3.cloned.1.call-update) | async-done | bytes 8388624 | tf_op jit(solution)/shard_map/all_gather | solution.py:189
  376.1 8.3 %copy.42 = f32[4,8,32,2048]{3,2,1,0:T(8,128)S(1)} copy(f32[4,8,32,2048]{3,1,2,0:T(8,128)} %bitcast.103) | data formatting | bytes 16777216
  384.4 1.3 bitcast_reduce_fusion
  385.7 0.7 broadcast_multiply_fusion
  386.4 3.8 all-to-all-start.3
  390.3 9.1 %fusion.45 = bf16[1,2048,768]{2,1,0:T(8,128)(2,1)} fusion(bf16[1152,768]{1,0:T(8,128)(2,1)} %copy-done.10, bf16[1152,4096]{1,0:T(8,128)(2,1)} %reshape.117), kind=kOutput, calls=%fused_computation.55 | convolution fusion | flops 3625451520 | bytes 9633792 | tf_op jit(solution)/shard_map/dot_general | solution.py:93
  399.4 9.1 %fusion.41 = bf16[1,768,2048]{2,1,0:T(8,128)(2,1)} fusion(bf16[1,1152,768]{2,1,0:T(8,128)(2,1)S(1)} %copy-done.5, bf16[1,1152,768]{2,1,0:T(8,128)(2,1)S(1)} %copy-done.7, f32[1152]{0:T(1024)S(1)} %reshape.121, bf16[1152,4096]{1,0:T(8,128)(2,1)} %reshape.117), kind=kOutput, calls=%fused_computation.53 | convolution fusion | flops 3639607296 | bytes 11407872 | tf_op jit(solution)/shard_map/dot_general | solution.py:99
  408.5 6.3 %fusion.42 = bf16[1,2048,768]{2,1,0:T(8,128)(2,1)} fusion(bf16[1152,4096]{1,0:T(8,128)(2,1)S(1)} %bitcast.102, f32[1152,768]{1,0:T(8,128)S(1)} %copy-done.9, bf16[1,1152,768]{2,1,0:T(8,128)(2,1)S(1)} %copy-done.7), kind=kOutput, calls=%fused_computation.54 | convolution fusion | flops 3631644672 | bytes 13172736 | tf_op jit(solution)/shard_map/dot_general | solution.py:96
  414.8 92.9 %all-to-all-done.3 = bf16[32,36,2048]{2,1,0:T(8,128)(2,1)} async-done(((bf16[32,36,2048]{2,1,0:T(8,128)(2,1)}), bf16[32,36,2048]{2,1,0:T(8,128)(2,1)}, u32[]{:S(2)}, u32[]{:S(2)}) %all-to-all-start.3) | async-done | bytes 4718624 | tf_op jit(solution)/shard_map/all_to_all | solution.py:193
  507.7 7.4 %reshape.120 = bf16[1152,2048]{1,0:T(8,128)(2,1)} reshape(bf16[32,36,2048]{2,1,0:T(8,128)(2,1)} %all-to-all-done.3) | data formatting | bytes 9437184 | tf_op jit(solution)/shard_map/reshape | solution.py:195
  515.1 3.2 fusion.76
  518.4 1.1 fusion.50
  (34 shorter events, 0.3 us)
Async XLA Ops:
  7.2 314.4 %copy-start = (bf16[1,2048,768]{2,1,0:T(8,128)(2,1)S(1)}, bf16[1,2048,768]{2,1,0:T(8,128)(2,1)}, u32[]{:S(2)}) copy-start(bf16[1,2048,768]{2,1,0:T(8,128)(2,1)} %param.15) | copy-start | bytes 9437188
  24.4 8.8 %copy-start.3 = (s32[128,8]{0,1:T(8,128)S(1)}, s32[128,8]{0,1:T(8,128)}, u32[]{:S(2)}) copy-start(s32[128,8]{0,1:T(8,128)} %param.11) | copy-start | bytes 12292
  24.4 237.3 %all-to-all-start = ((bf16[32,36,4096]{2,1,0:T(8,128)(2,1)}), bf16[32,36,4096]{2,1,0:T(8,128)(2,1)}, u32[]{:S(2)}, u32[]{:S(2)}) async-start(bf16[32,36,4096]{2,1,0:T(8,128)(2,1)} %convolution_convert_fusion), calls=%async_computation | async-start | bytes 20971520 | tf_op jit(solution)/shard_map/all_to_all | solution.py:159
  284.3 9.6 %all-to-all-start.1 = ((bf16[32,1,36]{2,1,0:T(2,128)(2,1)}), bf16[32,1,36]{2,1,0:T(2,128)(2,1)S(1)}, u32[]{:S(2)}, u32[]{:S(2)}) async-start(bf16[32,1,36]{2,1,0:T(2,128)(2,1)} %convert_element_type.152), calls=%async_computation.1 | async-start | bytes 32768 | tf_op jit(solution)/shard_map/all_to_all | solution.py:175
  286.9 89.2 %all-gather.3.cloned.1.call-start = ((), (), s32[]{:S(2)}) async-start(), calls=%async_computation.4 | async-start | bytes 8650752 | tf_op jit(solution)/shard_map/all_gather | solution.py:189
  321.6 6.3 %copy-start.10 = (bf16[1152,768]{1,0:T(8,128)(2,1)}, bf16[1152,768]{1,0:T(8,128)(2,1)S(1)}, u32[]{:S(2)}) copy-start(bf16[1152,768]{1,0:T(8,128)(2,1)S(1)} %get-tuple-element.11) | copy-start | bytes 5308420
  321.6 6.4 %copy-start.8 = (f32[1152,768]{1,0:T(8,128)}, f32[1152,768]{1,0:T(8,128)S(1)}, u32[]{:S(2)}) copy-start(f32[1152,768]{1,0:T(8,128)S(1)} %get-tuple-element.12) | copy-start | bytes 10616836
  321.6 6.4 %copy-start.4 = (bf16[1,2048,768]{2,1,0:T(8,128)(2,1)S(1)}, bf16[1,2048,768]{2,1,0:T(8,128)(2,1)}, u32[]{:S(2)}) copy-start(bf16[1,2048,768]{2,1,0:T(8,128)(2,1)} %param.16) | copy-start | bytes 9437188
  321.6 6.4 %copy-start.6 = (bf16[1,1152,768]{2,1,0:T(8,128)(2,1)S(1)}, bf16[1,1152,768]{2,1,0:T(8,128)(2,1)}, u32[]{:S(2)}) copy-start(bf16[1,1152,768]{2,1,0:T(8,128)(2,1)} %param.13) | copy-start | bytes 5308420
  386.4 121.3 %all-to-all-start.3 = ((bf16[32,36,2048]{2,1,0:T(8,128)(2,1)}), bf16[32,36,2048]{2,1,0:T(8,128)(2,1)}, u32[]{:S(2)}, u32[]{:S(2)}) async-start(bf16[32,36,2048]{2,1,0:T(8,128)(2,1)} %reshape.119), calls=%async_computation.3 | async-start | bytes 10485760 | tf_op jit(solution)/shard_map/all_to_all | solution.py:193
  390.2 9.1 %copy-start.5 = (bf16[1,1152,768]{2,1,0:T(8,128)(2,1)S(1)}, bf16[1,1152,768]{2,1,0:T(8,128)(2,1)}, u32[]{:S(2)}) copy-start(bf16[1,1152,768]{2,1,0:T(8,128)(2,1)} %param.14) | copy-start | bytes 5308420
  390.2 9.1 %copy-start.7 = (bf16[1,1152,768]{2,1,0:T(8,128)(2,1)S(1)}, bf16[1,1152,768]{2,1,0:T(8,128)(2,1)}, u32[]{:S(2)}) copy-start(bf16[1,1152,768]{2,1,0:T(8,128)(2,1)} %param.13) | copy-start | bytes 5308420
  390.3 18.2 %slice-start = ((s8[9437184]{0:T(1024)(128)(4,1)}), s8[4194304]{0:T(1024)(128)(4,1)S(1)}, s32[]{:S(2)}) async-start(s8[9437184]{0:T(1024)(128)(4,1)} %bitcast.101), calls=%async_computation.5 | async-start | bytes 8388608
  390.3 18.2 %slice-start.1 = ((s8[9437184]{0:T(1024)(128)(4,1)}), s8[4194304]{0:T(1024)(128)(4,1)S(1)}, s32[]{:S(2)}) async-start(s8[9437184]{0:T(1024)(128)(4,1)} %bitcast.101), calls=%async_computation.6 | async-start | bytes 8388608
  399.3 9.1 %slice-start.2 = ((s8[9437184]{0:T(1024)(128)(4,1)}), s8[1048576]{0:T(1024)(128)(4,1)S(1)}, s32[]{:S(2)}) async-start(s8[9437184]{0:T(1024)(128)(4,1)} %bitcast.101), calls=%async_computation.7 | async-start | bytes 2097152
  399.3 9.1 %copy-start.9 = (f32[1152,768]{1,0:T(8,128)S(1)}, f32[1152,768]{1,0:T(8,128)}, u32[]{:S(2)}) copy-start(f32[1152,768]{1,0:T(8,128)} %copy-done.8) | copy-start | bytes 10616836
  507.7 11.8 %copy-start.1 = (bf16[1,2048,768]{2,1,0:T(8,128)(2,1)S(1)}, bf16[1,2048,768]{2,1,0:T(8,128)(2,1)}, u32[]{:S(2)}) copy-start(bf16[1,2048,768]{2,1,0:T(8,128)(2,1)} %param.15) | copy-start | bytes 9437188
  515.1 3.3 copy-start.2
Sparse Core Ops, SparseCore 0:
  302.3 73.7 all-gather.2
